TPU v7x, 256 devices: a whole 4x4x8 slice. The times are simulated.
256 devices in a mesh: src: 16 (over y, x), tgt: 16 (over z, core).
Axes of the slice: x: 4, y: 4, z: 8, core: 2. Of those that a mesh axis runs over, the one named last changes fastest.
Arguments:
- src_emb_t: bfloat16 [300, 16384], P(None, 'src'), may hold values from -6 to 6
- tgt_emb_t: bfloat16 [300, 32768], P(None, 'tgt'), may hold values from -6 to 6
- core: float32 [300, 300], replicated, may hold values from -0.08 to 0.2
- src_logw: float32 [16384], P('src'), may hold values from -1.5 to 1.5
- tgt_logw: float32 [32768], P('tgt'), may hold values from -1.5 to 1.5
Outputs:
- src_potential: float32 [16384], P('src')
- tgt_potential: float32 [32768], P('tgt')
- next_core: float32 [300, 300], replicated
All inputs are finite; a program needn't handle non-finite values.
Results may differ from a plain program's by a relative error of at most 0.0036.
Values sent between devices are 32-bit elements; how exact they have to be, the bound alone decides.
No kernel may reach another device: no remote copies, remote signals or barrier semaphores. Data moves between devices by JAX's collectives and lax.ppermute only.
A program may use at most 64 MiB of HBM per device.

v0:
```python
import jax
import jax.numpy as jnp
from jax import lax
from jax.sharding import PartitionSpec as P

D = 300
ITERS = 3


def row_lse(shifted):
    peaks = jnp.max(shifted, axis=1)
    peaks = lax.pmax(peaks, "tgt")
    totals = lax.psum(jnp.sum(jnp.exp(shifted - peaks[:, None]), axis=1), "tgt")
    return peaks + jnp.log(totals)


def col_lse(shifted):
    peaks = jnp.max(shifted, axis=0)
    peaks = lax.pmax(peaks, "src")
    totals = lax.psum(jnp.sum(jnp.exp(shifted - peaks[None, :]), axis=0), "src")
    return peaks + jnp.log(totals)


def per_device(src_emb_t, tgt_emb_t, core, src_logw, tgt_logw):
    projected = jnp.dot(
        core.T, src_emb_t.astype(jnp.float32), precision=lax.Precision.HIGHEST
    ).astype(jnp.bfloat16)

    def scores_of():
        return lax.dot_general(
            projected, tgt_emb_t, (((0,), (0,)), ((), ())), preferred_element_type=jnp.float32
        )

    stored = scores_of()
    tgt_pot = jnp.zeros((tgt_emb_t.shape[1],), jnp.float32)
    src_pot = jnp.zeros((src_emb_t.shape[1],), jnp.float32)
    for step in range(ITERS):
        current = stored if step == 0 else scores_of()
        src_pot = src_logw - row_lse(current + tgt_pot[None, :])
        current = scores_of()
        tgt_pot = tgt_logw - col_lse(current + src_pot[:, None])
    current = scores_of()
    plan = jnp.exp(current + src_pot[:, None] + tgt_pot[None, :]).astype(jnp.bfloat16)
    total_words = src_emb_t.shape[1] * lax.axis_size("src")
    share = src_emb_t.shape[1] // lax.axis_size("tgt")
    portion = lax.psum_scatter(
        lax.dot_general(
            plan, tgt_emb_t, (((1,), (1,)), ((), ())), preferred_element_type=jnp.float32
        ),
        "tgt",
        scatter_dimension=0,
        tiled=True,
    )
    offset = lax.axis_index("tgt") * share
    my_words = lax.dynamic_slice_in_dim(src_emb_t, offset, share, 1)
    partial_core = jnp.dot(my_words.astype(jnp.float32), portion, precision=lax.Precision.HIGHEST)
    summed = lax.psum(partial_core, ("src", "tgt"))
    next_core = summed * (D / total_words)
    return (src_pot, tgt_pot, next_core)


def solution(mesh):
    placed = (P(None, "src"), P(None, "tgt"), P(), P("src"), P("tgt"))
    return jax.shard_map(
        per_device, mesh=mesh, in_specs=placed, out_specs=(P("src"), P("tgt"), P()), check_vma=False
    )
```

profile of v0, /device:TPU:2, one launch (start us, length us, event | category | flops | bytes accessed | tf_op | source)
XLA Modules:
  0.0 762.6 jit_solution(15984662700582594350)
XLA Ops:
  7.2 0.0 copy-start
  7.2 0.0 reduce-scatter.2.cloned.1.call-start
  7.2 2.5 convolution_convert_fusion
  9.7 0.0 copy-done
  9.7 0.0 copy-start.3
  9.7 5.6 fusion.6
  15.4 28.8 %pmax.42 = f32[1024]{0:T(1024)S(1)} all-reduce(f32[1024]{0:T(1024)S(1)} %get-tuple-element.3), channel_id=1, replica_groups=mesh['src'=16,'tgt'=16] {'tgt'}, use_global_device_ids=true, to_apply=%region_1.0 | all-reduce | flops 1024 | bytes 8192 | tf_op jit(solution)/shard_map/pmax | solution.py:12
  44.2 4.6 exponential_reduce_fusion.5
  48.8 23.6 %psum.49 = f32[1024]{0:T(1024)S(1)} all-reduce(f32[1024]{0:T(1024)S(1)} %exponential_reduce_fusion.5), channel_id=1, replica_groups=mesh['src'=16,'tgt'=16] {'tgt'}, use_global_device_ids=true, to_apply=%region_3.0 | all-reduce | flops 1024 | bytes 8192 | tf_op jit(solution)/shard_map/psum | solution.py:13
  72.4 0.0 copy-done.3
  72.4 0.0 copy-start.1
  72.4 4.0 add_reduce_fusion.3
  76.4 37.2 %pmax.43 = f32[2048]{0:T(1024)S(1)} all-reduce(f32[2048]{0:T(1024)S(1)} %add_reduce_fusion.3), channel_id=1, replica_groups=mesh['src'=16,'tgt'=16] {'src'}, use_global_device_ids=true, to_apply=%region_5.0 | all-reduce | flops 2048 | bytes 16384 | tf_op jit(solution)/shard_map/pmax | solution.py:19
  113.6 4.3 exponential_reduce_fusion.4
  117.9 40.5 %psum.50 = f32[2048]{0:T(1024)S(1)} all-reduce(f32[2048]{0:T(1024)S(1)} %exponential_reduce_fusion.4), channel_id=1, replica_groups=mesh['src'=16,'tgt'=16] {'src'}, use_global_device_ids=true, to_apply=%region_7.0 | all-reduce | flops 2048 | bytes 16384 | tf_op jit(solution)/shard_map/psum | solution.py:20
  158.4 0.0 copy-done.1
  158.4 4.0 add_reduce_fusion.2
  162.4 23.6 %pmax.44 = f32[1024]{0:T(1024)S(1)} all-reduce(f32[1024]{0:T(1024)S(1)} %add_reduce_fusion.2), channel_id=1, replica_groups=mesh['src'=16,'tgt'=16] {'tgt'}, use_global_device_ids=true, to_apply=%region_9.0 | all-reduce | flops 1024 | bytes 8192 | tf_op jit(solution)/shard_map/pmax | solution.py:12
  186.0 4.4 exponential_reduce_fusion.3
  190.4 23.6 %psum.51 = f32[1024]{0:T(1024)S(1)} all-reduce(f32[1024]{0:T(1024)S(1)} %exponential_reduce_fusion.3), channel_id=1, replica_groups=mesh['src'=16,'tgt'=16] {'tgt'}, use_global_device_ids=true, to_apply=%region_11.0 | all-reduce | flops 1024 | bytes 8192 | tf_op jit(solution)/shard_map/psum | solution.py:13
  213.9 4.0 add_reduce_fusion.1
  217.9 36.0 %pmax.45 = f32[2048]{0:T(1024)S(1)} all-reduce(f32[2048]{0:T(1024)S(1)} %add_reduce_fusion.1), channel_id=1, replica_groups=mesh['src'=16,'tgt'=16] {'src'}, use_global_device_ids=true, to_apply=%region_13.0 | all-reduce | flops 2048 | bytes 16384 | tf_op jit(solution)/shard_map/pmax | solution.py:19
  253.9 4.3 exponential_reduce_fusion.2
  258.2 38.0 %psum.52 = f32[2048]{0:T(1024)S(1)} all-reduce(f32[2048]{0:T(1024)S(1)} %exponential_reduce_fusion.2), channel_id=1, replica_groups=mesh['src'=16,'tgt'=16] {'src'}, use_global_device_ids=true, to_apply=%region_15.0 | all-reduce | flops 2048 | bytes 16384 | tf_op jit(solution)/shard_map/psum | solution.py:20
  296.2 4.0 add_reduce_fusion
  300.2 23.7 %pmax.46 = f32[1024]{0:T(1024)S(1)} all-reduce(f32[1024]{0:T(1024)S(1)} %add_reduce_fusion), channel_id=1, replica_groups=mesh['src'=16,'tgt'=16] {'tgt'}, use_global_device_ids=true, to_apply=%region_17.0 | all-reduce | flops 1024 | bytes 8192 | tf_op jit(solution)/shard_map/pmax | solution.py:12
  324.0 4.4 exponential_reduce_fusion.1
  328.3 23.6 %psum.53 = f32[1024]{0:T(1024)S(1)} all-reduce(f32[1024]{0:T(1024)S(1)} %exponential_reduce_fusion.1), channel_id=1, replica_groups=mesh['src'=16,'tgt'=16] {'tgt'}, use_global_device_ids=true, to_apply=%region_19.0 | all-reduce | flops 1024 | bytes 8192 | tf_op jit(solution)/shard_map/psum | solution.py:13
  351.9 0.0 copy-start.2
  351.9 4.0 add_reduce_fusion.4
  355.9 36.0 %pmax.47 = f32[2048]{0:T(1024)S(1)} all-reduce(f32[2048]{0:T(1024)S(1)} %add_reduce_fusion.4), channel_id=1, replica_groups=mesh['src'=16,'tgt'=16] {'src'}, use_global_device_ids=true, to_apply=%region_21.0 | all-reduce | flops 2048 | bytes 16384 | tf_op jit(solution)/shard_map/pmax | solution.py:19
  391.9 4.3 exponential_reduce_fusion
  396.2 38.0 %psum.54 = f32[2048]{0:T(1024)S(1)} all-reduce(f32[2048]{0:T(1024)S(1)} %exponential_reduce_fusion), channel_id=1, replica_groups=mesh['src'=16,'tgt'=16] {'src'}, use_global_device_ids=true, to_apply=%region_23.0 | all-reduce | flops 2048 | bytes 16384 | tf_op jit(solution)/shard_map/psum | solution.py:20
  434.2 0.0 copy-done.2
  434.2 0.0 copy-start.4
  434.2 7.0 fusion
  441.2 0.0 copy-done.4
  441.2 0.0 reduce-scatter.2.cloned.1.call-update
  441.3 0.0 all-reduce.2.cloned.1.call-start
  441.3 52.7 %reduce-scatter.2.cloned.1.call-done = f32[64,300]{1,0:T(8,128)} async-done(((f32[1024,300]{1,0:T(8,128)}), f32[64,300]{1,0:T(8,128)}) %reduce-scatter.2.cloned.1.call-update) | async-done | bytes 76816 | tf_op jit(solution)/shard_map/reduce_scatter | solution.py:46
  494.0 2.1 fusion.3
  496.1 0.0 all-reduce.2.cloned.1.call-update
  496.1 257.8 %all-reduce.2.cloned.1.call-done = f32[300,300]{1,0:T(8,128)} async-done(((f32[300,300]{1,0:T(8,128)}), f32[300,300]{1,0:T(8,128)}) %all-reduce.2.cloned.1.call-update) | async-done | bytes 360016 | tf_op jit(solution)/shard_map/psum | solution.py:57
  753.9 1.8 broadcast_multiply_fusion
  (6 shorter events, 0.1 us)
Async XLA Ops:
  7.2 2.5 copy-start
  7.2 486.8 %reduce-scatter.2.cloned.1.call-start = ((), (), s32[]{:S(2)}) async-start(), calls=%async_computation.1 | async-start | bytes 1671168 | tf_op jit(solution)/shard_map/reduce_scatter | solution.py:46
  9.7 62.6 %copy-start.3 = (f32[1024]{0:T(1024)S(1)}, f32[1024]{0:T(1024)}, u32[]{:S(2)}) copy-start(f32[1024]{0:T(1024)} %param.8) | copy-start | bytes 12292
  72.4 86.0 %copy-start.1 = (f32[2048]{0:T(1024)S(1)}, f32[2048]{0:T(1024)}, u32[]{:S(2)}) copy-start(f32[2048]{0:T(1024)} %param.9) | copy-start | bytes 24580
  351.9 82.3 %copy-start.2 = (f32[1024]{0:T(1024)}, f32[1024]{0:T(1024)S(1)}, u32[]{:S(2)}) copy-start(f32[1024]{0:T(1024)S(1)} %add_subtract_fusion.3) | copy-start | bytes 12292
  434.2 7.0 copy-start.4
  441.3 312.7 %all-reduce.2.cloned.1.call-start = ((), (), s32[]{:S(2)}) async-start(), calls=%async_computation.2 | async-start | bytes 933888 | tf_op jit(solution)/shard_map/psum | solution.py:57
Sparse Core Ops, SparseCore 0:
  441.4 52.5 reduce-scatter.1
  500.1 253.7 all-reduce.1
where the time goes:
time: 763 us
  blocking collectives  372 us (49%)
  waiting for transfers between devices  311 us (41%)
  other arithmetic  48.2 us (6%)
  matrix products  17.2 us (2%)
  between operations  14.3 us (2%)
    psum x1, waiting for transfers between devices, per_device(): summed = lax.psum(partial_core, ('src', 'tgt'))  258 us
    psum x3, blocking collectives, col_lse(): totals = lax.psum(jnp.sum(jnp.exp(shifted - peaks[None, :]), axis=0), 'src')  116 us
    pmax x3, blocking collectives, col_lse(): peaks = lax.pmax(peaks, 'src')  109 us
    pmax x3, blocking collectives, row_lse(): peaks = lax.pmax(peaks, 'tgt')  76.1 us
    psum x3, blocking collectives, row_lse(): totals = lax.psum(jnp.sum(jnp.exp(shifted - peaks[:, None]), axis=1), 'tgt')  70.7 us
    reduce_scatter x1, waiting for transfers between devices, per_device(): lax.psum_scatter(lax.dot_general(plan, tgt_emb_t, (((1,), (1,)), ((), ())...  52.7 us
  transfers between devices with their start and end apart: 2, of which 2 were waited for; matrix products, arithmetic and copies ran while one was open for 0% of the time, Pallas kernels for 0%

commit v1 on v0

--- a/solution.py
+++ b/solution.py
@@ -10,7 +10,9 @@
 def row_lse(shifted):
     peaks = jnp.max(shifted, axis=1)
     peaks = lax.pmax(peaks, "tgt")
-    totals = lax.psum(jnp.sum(jnp.exp(shifted - peaks[:, None]), axis=1), "tgt")
+    totals = jnp.sum(
+        lax.all_gather(jnp.sum(jnp.exp(shifted - peaks[:, None]), axis=1), "tgt"), axis=0
+    )
     return peaks + jnp.log(totals)
 
 

time: 763 us -> 736 us (0.965)
  blocking collectives: 372 us -> 345 us
    psum x3 -> x0, blocking collectives: 70.7 us -> none  [row_lse(): totals = lax.psum(jnp.sum(jnp.exp(shifted - peaks[:, None]), axis=1), 'tgt')]
    all_gather x0 -> x3, blocking collectives: none -> 43 us  [row_lse(): lax.all_gather(jnp.sum(jnp.exp(shifted - peaks[:, None]), axis=1), 'tgt')]
where the time goes in v1:
time: 736 us
  blocking collectives  345 us (47%)
  waiting for transfers between devices  311 us (42%)
  other arithmetic  48.2 us (7%)
  matrix products  17.2 us (2%)
  between operations  14.3 us (2%)
    psum x1, waiting for transfers between devices, per_device(): summed = lax.psum(partial_core, ('src', 'tgt'))  258 us
    psum x3, blocking collectives, col_lse(): totals = lax.psum(jnp.sum(jnp.exp(shifted - peaks[None, :]), axis=0), 'src')  117 us
    pmax x3, blocking collectives, col_lse(): peaks = lax.pmax(peaks, 'src')  109 us
    pmax x3, blocking collectives, row_lse(): peaks = lax.pmax(peaks, 'tgt')  76.1 us
    reduce_scatter x1, waiting for transfers between devices, per_device(): lax.psum_scatter(lax.dot_general(plan, tgt_emb_t, (((1,), (1,)), ((), ())...  53.2 us
    all_gather x3, blocking collectives, row_lse(): lax.all_gather(jnp.sum(jnp.exp(shifted - peaks[:, None]), axis=1), 'tgt')  43 us
  transfers between devices with their start and end apart: 2, of which 2 were waited for; matrix products, arithmetic and copies ran while one was open for 0% of the time, Pallas kernels for 0%

profile of v1, /device:TPU:2, one launch (start us, length us, event | category | flops | bytes accessed | tf_op | source)
XLA Modules:
  0.0 735.6 jit_solution(8679277646397729777)
XLA Ops:
  7.2 0.0 copy-start
  7.2 0.0 reduce-scatter.2.cloned.1.call-start
  7.2 2.5 convolution_convert_fusion
  9.7 0.0 copy-done
  9.7 0.0 copy-start.3
  9.7 5.6 fusion.6
  15.4 28.8 %pmax.42 = f32[1024]{0:T(1024)S(1)} all-reduce(f32[1024]{0:T(1024)S(1)} %get-tuple-element.3), channel_id=1, replica_groups=mesh['src'=16,'tgt'=16] {'tgt'}, use_global_device_ids=true, to_apply=%region_1.0 | all-reduce | flops 1024 | bytes 8192 | tf_op jit(solution)/shard_map/pmax | solution.py:12
  44.2 4.6 exponential_reduce_fusion.5
  48.8 14.3 %all-gather = f32[16384]{0:T(1024)S(1)} all-gather(f32[1024]{0:T(1024)S(1)} %exponential_reduce_fusion.5), channel_id=2, replica_groups=mesh['src'=16,'tgt'=16] {'tgt'}, dimensions={0}, use_global_device_ids=true | all-gather | bytes 69632 | tf_op jit(solution)/shard_map/all_gather | solution.py:14
  63.2 0.0 copy-done.3
  63.2 0.0 copy-start.1
  63.2 4.0 add_reduce_fusion.3
  67.2 37.2 %pmax.43 = f32[2048]{0:T(1024)S(1)} all-reduce(f32[2048]{0:T(1024)S(1)} %add_reduce_fusion.3), channel_id=1, replica_groups=mesh['src'=16,'tgt'=16] {'src'}, use_global_device_ids=true, to_apply=%region_5.0 | all-reduce | flops 2048 | bytes 16384 | tf_op jit(solution)/shard_map/pmax | solution.py:21
  104.4 4.3 exponential_reduce_fusion.4
  108.7 40.5 %psum.28 = f32[2048]{0:T(1024)S(1)} all-reduce(f32[2048]{0:T(1024)S(1)} %exponential_reduce_fusion.4), channel_id=1, replica_groups=mesh['src'=16,'tgt'=16] {'src'}, use_global_device_ids=true, to_apply=%region_7.0 | all-reduce | flops 2048 | bytes 16384 | tf_op jit(solution)/shard_map/psum | solution.py:22
  149.2 0.0 copy-done.1
  149.3 4.0 add_reduce_fusion.2
  153.3 23.6 %pmax.44 = f32[1024]{0:T(1024)S(1)} all-reduce(f32[1024]{0:T(1024)S(1)} %add_reduce_fusion.2), channel_id=1, replica_groups=mesh['src'=16,'tgt'=16] {'tgt'}, use_global_device_ids=true, to_apply=%region_9.0 | all-reduce | flops 1024 | bytes 8192 | tf_op jit(solution)/shard_map/pmax | solution.py:12
  176.8 4.4 exponential_reduce_fusion.3
  181.2 14.3 %all-gather.1 = f32[16384]{0:T(1024)S(1)} all-gather(f32[1024]{0:T(1024)S(1)} %exponential_reduce_fusion.3), channel_id=3, replica_groups=mesh['src'=16,'tgt'=16] {'tgt'}, dimensions={0}, use_global_device_ids=true | all-gather | bytes 69632 | tf_op jit(solution)/shard_map/all_gather | solution.py:14
  195.6 4.0 add_reduce_fusion.1
  199.6 35.9 %pmax.45 = f32[2048]{0:T(1024)S(1)} all-reduce(f32[2048]{0:T(1024)S(1)} %add_reduce_fusion.1), channel_id=1, replica_groups=mesh['src'=16,'tgt'=16] {'src'}, use_global_device_ids=true, to_apply=%region_13.0 | all-reduce | flops 2048 | bytes 16384 | tf_op jit(solution)/shard_map/pmax | solution.py:21
  235.5 4.3 exponential_reduce_fusion.2
  239.8 38.0 %psum.29 = f32[2048]{0:T(1024)S(1)} all-reduce(f32[2048]{0:T(1024)S(1)} %exponential_reduce_fusion.2), channel_id=1, replica_groups=mesh['src'=16,'tgt'=16] {'src'}, use_global_device_ids=true, to_apply=%region_15.0 | all-reduce | flops 2048 | bytes 16384 | tf_op jit(solution)/shard_map/psum | solution.py:22
  277.9 4.0 add_reduce_fusion
  281.9 23.7 %pmax.46 = f32[1024]{0:T(1024)S(1)} all-reduce(f32[1024]{0:T(1024)S(1)} %add_reduce_fusion), channel_id=1, replica_groups=mesh['src'=16,'tgt'=16] {'tgt'}, use_global_device_ids=true, to_apply=%region_17.0 | all-reduce | flops 1024 | bytes 8192 | tf_op jit(solution)/shard_map/pmax | solution.py:12
  305.6 4.4 exponential_reduce_fusion.1
  310.0 14.3 %all-gather.2 = f32[16384]{0:T(1024)S(1)} all-gather(f32[1024]{0:T(1024)S(1)} %exponential_reduce_fusion.1), channel_id=4, replica_groups=mesh['src'=16,'tgt'=16] {'tgt'}, dimensions={0}, use_global_device_ids=true | all-gather | bytes 69632 | tf_op jit(solution)/shard_map/all_gather | solution.py:14
  324.4 0.0 copy-start.2
  324.4 4.0 add_reduce_fusion.4
  328.4 36.0 %pmax.47 = f32[2048]{0:T(1024)S(1)} all-reduce(f32[2048]{0:T(1024)S(1)} %add_reduce_fusion.4), channel_id=1, replica_groups=mesh['src'=16,'tgt'=16] {'src'}, use_global_device_ids=true, to_apply=%region_21.0 | all-reduce | flops 2048 | bytes 16384 | tf_op jit(solution)/shard_map/pmax | solution.py:21
  364.4 4.3 exponential_reduce_fusion
  368.7 38.0 %psum.30 = f32[2048]{0:T(1024)S(1)} all-reduce(f32[2048]{0:T(1024)S(1)} %exponential_reduce_fusion), channel_id=1, replica_groups=mesh['src'=16,'tgt'=16] {'src'}, use_global_device_ids=true, to_apply=%region_23.0 | all-reduce | flops 2048 | bytes 16384 | tf_op jit(solution)/shard_map/psum | solution.py:22
  406.7 0.0 copy-done.2
  406.7 0.0 copy-start.4
  406.8 7.0 fusion
  413.8 0.0 copy-done.4
  413.8 0.0 reduce-scatter.2.cloned.1.call-update
  413.8 0.0 all-reduce.2.cloned.1.call-start
  413.8 53.2 %reduce-scatter.2.cloned.1.call-done = f32[64,300]{1,0:T(8,128)} async-done(((f32[1024,300]{1,0:T(8,128)}), f32[64,300]{1,0:T(8,128)}) %reduce-scatter.2.cloned.1.call-update) | async-done | bytes 76816 | tf_op jit(solution)/shard_map/reduce_scatter | solution.py:48
  467.0 2.1 fusion.3
  469.1 0.0 all-reduce.2.cloned.1.call-update
  469.2 257.8 %all-reduce.2.cloned.1.call-done = f32[300,300]{1,0:T(8,128)} async-done(((f32[300,300]{1,0:T(8,128)}), f32[300,300]{1,0:T(8,128)}) %all-reduce.2.cloned.1.call-update) | async-done | bytes 360016 | tf_op jit(solution)/shard_map/psum | solution.py:59
  726.9 1.8 broadcast_multiply_fusion
  (12 shorter events, 0.2 us)
Async XLA Ops:
  7.2 2.5 copy-start
  7.2 459.9 %reduce-scatter.2.cloned.1.call-start = ((), (), s32[]{:S(2)}) async-start(), calls=%async_computation.1 | async-start | bytes 1671168 | tf_op jit(solution)/shard_map/reduce_scatter | solution.py:48
  9.7 53.5 %copy-start.3 = (f32[1024]{0:T(1024)S(1)}, f32[1024]{0:T(1024)}, u32[]{:S(2)}) copy-start(f32[1024]{0:T(1024)} %param.8) | copy-start | bytes 12292
  63.2 86.1 %copy-start.1 = (f32[2048]{0:T(1024)S(1)}, f32[2048]{0:T(1024)}, u32[]{:S(2)}) copy-start(f32[2048]{0:T(1024)} %param.9) | copy-start | bytes 24580
  324.4 82.4 %copy-start.2 = (f32[1024]{0:T(1024)}, f32[1024]{0:T(1024)S(1)}, u32[]{:S(2)}) copy-start(f32[1024]{0:T(1024)S(1)} %add_subtract_fusion.3) | copy-start | bytes 12292
  406.7 7.0 copy-start.4
  413.8 313.1 %all-reduce.2.cloned.1.call-start = ((), (), s32[]{:S(2)}) async-start(), calls=%async_computation.2 | async-start | bytes 933888 | tf_op jit(solution)/shard_map/psum | solution.py:59
Sparse Core Ops, SparseCore 0:
  413.9 53.0 reduce-scatter.1
  473.1 253.7 all-reduce.1
